TPU v7x, 32 devices: a whole 2x2x4 slice. The times are simulated.
32 devices in a mesh: groups: 2 (over y), freq: 4 (over z), tile: 4 (over x, core).
Axes of the slice: x: 2, y: 2, z: 4, core: 2. Of those that a mesh axis runs over, the one named last changes fastest.
Arguments:
- traces: bfloat16 [640, 32, 16384], P('freq', 'groups', 'tile'), parts along dimension 1, may hold values from -6 to 6
- v_factors: bfloat16 [4, 2, 32, 64, 8, 256], P('freq', None, None, 'tile'), may hold values from -0.375 to 0.375
- u_factors: bfloat16 [4, 2, 32, 64, 8, 256], P('freq', None, 'tile'), may hold values from -0.25 to 0.25
- ranks: int32 [4, 32, 64], P('freq', None, 'tile'), may hold values from 1 to 8
Outputs:
- convolved: bfloat16 [640, 32, 8192], P('freq', 'groups', 'tile'), parts along dimension 1
There are 2 independent parts, one for each index of `groups`. A program takes and returns all parts, laid end to end along the dimension named above; an argument that names none is the same for every part. Nothing has to cross between parts.
All inputs are finite; a program needn't handle non-finite values.
Results may differ from a plain program's by a relative error of at most 0.0074.
Values may be sent and summed in bfloat16 or wider, within the bound.
No kernel may reach another device: no remote copies, remote signals or barrier semaphores. Data moves between devices by JAX's collectives and lax.ppermute only.
A program may use at most 192 MiB of HBM per device.

v0:
```python
import math
import jax
import jax.numpy as jnp
from jax import lax
from jax.sharding import PartitionSpec as P

NT = 640
F0 = 40
CHUNKS = 2


def twiddle(freq_ids, time_ids):
    turns = (F0 + freq_ids)[:, None] * time_ids[None, :] % NT
    angle = turns.astype(jnp.float32) * (2.0 * math.pi / NT)
    return (jnp.cos(angle).astype(jnp.bfloat16), jnp.sin(angle).astype(jnp.bfloat16))


def spread_over(weights, count):
    rows, cols = weights.shape
    kind = weights.dtype
    repeat_rows = (
        jnp.arange(rows * count, dtype=jnp.int32)[:, None] // count
        == jnp.arange(rows, dtype=jnp.int32)[None, :]
    ).astype(kind)
    repeat_cols = (
        jnp.arange(cols, dtype=jnp.int32)[:, None]
        == jnp.arange(cols * count, dtype=jnp.int32)[None, :] // count
    ).astype(kind)
    tall = jnp.dot(repeat_rows, weights, preferred_element_type=jnp.float32).astype(kind)
    wide = jnp.dot(tall, repeat_cols, preferred_element_type=jnp.float32)
    same = (
        jnp.arange(rows * count, dtype=jnp.int32)[:, None] % count
        == jnp.arange(cols * count, dtype=jnp.int32)[None, :] % count
    )
    return jnp.where(same, wide, jnp.float32(0.0)).astype(kind)


def per_device(traces, v_factors, u_factors, ranks):
    time_count = traces.shape[0]
    virtual_sources = traces.shape[1]
    source_count = traces.shape[2]
    freq_local = v_factors.shape[0]
    freq_total = freq_local * lax.axis_size("freq")
    tile_width = v_factors.shape[5]
    rank_positions = v_factors.shape[4]
    rows_all = v_factors.shape[2]
    columns = v_factors.shape[3]
    time_ids = lax.axis_index("freq") * time_count + jnp.arange(time_count, dtype=jnp.int32)
    scale_time = 1.0 / math.sqrt(NT)
    freq_ids = jnp.arange(freq_total, dtype=jnp.int32)
    cosine, sine = twiddle(freq_ids, time_ids)
    chunks = CHUNKS if virtual_sources % CHUNKS == 0 else 1
    width = virtual_sources // chunks
    forward = spread_over(jnp.stack([cosine, -sine], 1).reshape(freq_total * 2, time_count), width)
    emitter_factors = v_factors[0]
    receiver_factors = u_factors[0]
    rank_mask = (
        jnp.arange(rank_positions, dtype=jnp.int32)[None, None, :, None]
        < ranks[0][:, :, None, None]
    )

    def source_product(left_operand_factors, right_operand_factors):
        return jnp.einsum(
            "ajrs,vjs->ajrv",
            left_operand_factors,
            right_operand_factors,
            preferred_element_type=jnp.float32,
        )

    def receiver_product(left_operand_factors, right_operand_factors):
        return jnp.einsum(
            "mdlh,mdlu->umh",
            left_operand_factors,
            right_operand_factors,
            preferred_element_type=jnp.float32,
        )

    sums = []
    for part in range(chunks):
        flat_traces = traces[:, part * width : (part + 1) * width, :].reshape(
            time_count * width, source_count
        )
        partial = jnp.dot(forward, flat_traces, preferred_element_type=jnp.float32).reshape(
            freq_total, 2, width, source_count
        )
        sums.append(lax.psum_scatter(partial, "freq", scatter_dimension=0, tiled=True))
    pieces = []
    for part in range(chunks):
        summed = sums[part]
        if pieces:
            summed, pieces[-1] = lax.optimization_barrier((summed, pieces[-1]))
        spectrum = (summed * scale_time).astype(jnp.bfloat16)[0]
        spectral_tiles = spectrum.reshape(2, width, columns, tile_width)
        real_coeff = source_product(emitter_factors[0], spectral_tiles[0]) - source_product(
            emitter_factors[1], spectral_tiles[1]
        )
        imag_coeff = source_product(emitter_factors[0], spectral_tiles[1]) + source_product(
            emitter_factors[1], spectral_tiles[0]
        )
        stacked = jnp.stack([real_coeff, imag_coeff])
        coefficients = jnp.where(rank_mask[None], stacked, jnp.float32(0.0)).astype(jnp.bfloat16)
        coefficients = coefficients.reshape(2, rows_all, columns, rank_positions * width)
        arrived = lax.all_to_all(coefficients, "tile", split_axis=1, concat_axis=2, tiled=True)
        rows_local = arrived.shape[1]
        columns_all = arrived.shape[2]
        arrived = arrived.reshape(2, rows_local, columns_all, rank_positions, width)
        real_recv = receiver_product(receiver_factors[0], arrived[0]) - receiver_product(
            receiver_factors[1], arrived[1]
        )
        imag_recv = receiver_product(receiver_factors[0], arrived[1]) + receiver_product(
            receiver_factors[1], arrived[0]
        )
        receivers = rows_local * tile_width
        received = (
            jnp.stack([real_recv, imag_recv]).reshape(1, 2, width, receivers).astype(jnp.bfloat16)
        )
        pieces.append(lax.all_gather(received, "freq", axis=0, tiled=True))
    piece = jnp.concatenate(pieces, axis=2)
    count = piece.shape[0]
    backward = jnp.stack([cosine.T, -sine.T], 2).reshape(time_count, count * 2)
    added = jnp.dot(
        spread_over(backward, virtual_sources),
        piece.reshape(count * 2 * virtual_sources, receivers),
        preferred_element_type=jnp.float32,
    )
    scale_freq = 1.0 / math.sqrt(freq_total)
    return (added * scale_freq).astype(jnp.bfloat16).reshape(time_count, virtual_sources, receivers)


def solution(mesh):
    placed = (
        P("freq", "groups", "tile"),
        P("freq", None, None, "tile", None, None),
        P("freq", None, "tile", None, None, None),
        P("freq", None, "tile"),
    )
    return jax.shard_map(
        per_device,
        mesh=mesh,
        in_specs=placed,
        out_specs=P("freq", "groups", "tile"),
        check_vma=False,
    )
```

profile of v0, /device:TPU:0, one launch (start us, length us, event | category | flops | bytes accessed | tf_op | source)
XLA Modules:
  0.0 136.0 jit_solution(8641000433981534925)
XLA Ops:
  6.9 0.4 fusion.7
  7.3 6.9 %fusion = f32[4,2,8,4096]{3,2,1,0:T(8,128)} fusion(bf16[4,2,8,1280]{3,2,1,0:T(8,128)(2,1)S(1)} %bitcast.242, bf16[160,16,4096]{2,1,0:T(8,128)(2,1)} %param.4), kind=kOutput, calls=%fused_computation.1 | convolution fusion | flops 671088640 | bytes 11698176 | tf_op jit(solution)/shard_map/dot_general | solution.py:83
  14.3 6.9 %fusion.2 = f32[4,2,8,4096]{3,2,1,0:T(8,128)} fusion(bf16[4,2,8,1280]{3,2,1,0:T(8,128)(2,1)S(1)} %bitcast.243, bf16[160,16,4096]{2,1,0:T(8,128)(2,1)} %param.4), kind=kOutput, calls=%fused_computation.3 | convolution fusion | flops 671088640 | bytes 11698176 | tf_op jit(solution)/shard_map/dot_general | solution.py:83
  21.6 0.2 copy.70
  21.9 5.1 %fusion.83 = (bf16[1,1,32,16,8,256]{5,4,3,2,1,0:T(8,128)(2,1)}, bf16[1,1,32,16,8,256]{5,4,3,2,1,0:T(8,128)(2,1)}) fusion(bf16[1,2,32,16,8,256]{5,4,3,2,1,0:T(8,128)(2,1)} %param.5), kind=kLoop, calls=%fused_computation.135 | loop fusion | bytes 8388608 | tf_op jit(solution)/shard_map/slice | solution.py:95
  27.0 1.7 %fusion.82 = (bf16[1,1,8,64,8,256]{5,4,3,2,1,0:T(8,128)(2,1)S(1)}, bf16[1,1,8,64,8,256]{5,4,3,2,1,0:T(8,128)(2,1)}) fusion(bf16[1,2,8,64,8,256]{5,4,3,2,1,0:T(8,128)(2,1)S(1)} %copy-done.5), kind=kLoop, calls=%fused_computation.134 | loop fusion | bytes 8388608 | tf_op jit(solution)/shard_map/slice | solution.py:107
  28.6 1.4 %convolution_convert_fusion = bf16[2560,8]{0,1:T(8,128)(2,1)S(1)} fusion(bf16[160,8]{0,1:T(8,128)(2,1)S(1)} %reshape.600, s32[2560]{0:T(1024)S(1)} %add_select_fusion), kind=kOutput, calls=%fused_computation.9 | convolution fusion | flops 6983680 | bytes 53760 | tf_op jit(solution)/shard_map/dot_general | solution.py:29
  30.0 14.2 %reduce-scatter.5.cloned.1.call-done = f32[1,2,8,4096]{3,2,1,0:T(8,128)} async-done(((f32[4,2,8,4096]{3,2,1,0:T(8,128)}), f32[1,2,8,4096]{3,2,1,0:T(8,128)}) %reduce-scatter.5.cloned.1.call-update) | async-done | bytes 262160 | tf_op jit(solution)/shard_map/reduce_scatter | solution.py:86
  44.2 1.1 multiply_convert_fusion.2
  45.4 3.2 %fusion.10 = f32[16,8,32,8]{2,1,3,0:T(8,128)S(1)} fusion(bf16[8,16,256,1]{2,0,3,1:T(8,128)(2,1)S(1)} %bitcast.229, bf16[1,1,32,16,8,256]{5,4,3,2,1,0:T(8,128)(2,1)} %get-tuple-element.12), kind=kOutput, calls=%fused_computation.19 | convolution fusion | flops 16777216 | bytes 2293760 | tf_op jit(solution)/shard_map/ajrs,vjs->ajrv/dot_general | solution.py:63
  48.6 1.5 %fusion.11 = f32[16,8,32,8]{2,1,3,0:T(8,128)S(1)} fusion(bf16[8,16,256,1]{2,0,3,1:T(8,128)(2,1)S(1)} %bitcast.233, bf16[1,1,32,16,8,256]{5,4,3,2,1,0:T(8,128)(2,1)S(1)} %copy-done.3), kind=kOutput, calls=%fused_computation.20 | convolution fusion | flops 16777216 | bytes 2293760 | tf_op jit(solution)/shard_map/ajrs,vjs->ajrv/dot_general | solution.py:63
  50.1 1.5 %fusion.28 = bf16[1,32,16,64]{1,3,2,0:T(8,128)(2,1)S(1)} fusion(f32[16,8,32,8]{2,1,3,0:T(8,128)S(1)} %fusion.10, bf16[8,16,256,1]{2,0,3,1:T(8,128)(2,1)S(1)} %bitcast.234, bf16[1,1,32,16,8,256]{5,4,3,2,1,0:T(8,128)(2,1)S(1)} %copy-done.1), kind=kOutput, calls=%fused_computation.37 | convolution fusion | flops 16842752 | bytes 2359296 | tf_op jit(solution)/shard_map/ajrs,vjs->ajrv/dot_general | solution.py:63
  51.6 0.2 copy.74
  51.8 3.1 %fusion.26 = bf16[1,32,16,64]{1,3,2,0:T(8,128)(2,1)S(1)} fusion(f32[16,8,32,8]{2,1,3,0:T(8,128)S(1)} %fusion.11, bf16[8,16,256,1]{2,0,3,1:T(8,128)(2,1)S(1)} %bitcast.230, bf16[1,1,32,16,8,256]{5,4,3,2,1,0:T(8,128)(2,1)} %get-tuple-element.11), kind=kOutput, calls=%fused_computation.35 | convolution fusion | flops 16842752 | bytes 2359296 | tf_op jit(solution)/shard_map/ajrs,vjs->ajrv/dot_general | solution.py:63
  54.9 0.2 copy.73
  55.2 0.9 reshape.620
  56.1 3.5 %all-to-all-start = ((bf16[4,2,8192]{2,1,0:T(2,128)(2,1)}), bf16[4,2,8192]{2,1,0:T(2,128)(2,1)S(1)}, u32[]{:S(2)}, u32[]{:S(2)}) async-start(bf16[4,2,8192]{2,1,0:T(2,128)(2,1)} %reshape.620), calls=%async_computation.2 | async-start | bytes 262144 | tf_op jit(solution)/shard_map/all_to_all | solution.py:103
  59.6 4.4 %all-to-all-done = bf16[4,2,8192]{2,1,0:T(2,128)(2,1)S(1)} async-done(((bf16[4,2,8192]{2,1,0:T(2,128)(2,1)}), bf16[4,2,8192]{2,1,0:T(2,128)(2,1)S(1)}, u32[]{:S(2)}, u32[]{:S(2)}) %all-to-all-start) | async-done | bytes 131104 | tf_op jit(solution)/shard_map/all_to_all | solution.py:103
  64.0 0.2 reshape.621
  64.3 0.3 copy.78
  64.6 0.3 squeeze.30
  64.9 0.3 copy.76
  65.2 0.3 squeeze.28
  65.5 2.2 %fusion.34 = f32[8,8,256]{2,1,0:T(8,128)S(1)} fusion(bf16[8,64,8,8]{1,3,2,0:T(8,128)(2,1)S(1)} %squeeze.28, bf16[1,1,8,64,8,256]{5,4,3,2,1,0:T(8,128)(2,1)} %get-tuple-element.10), kind=kOutput, calls=%fused_computation.43 | convolution fusion | flops 16777216 | bytes 2228224 | tf_op jit(solution)/shard_map/mdlh,mdlu->umh/dot_general | solution.py:71
  67.8 0.5 fusion.33
  68.3 0.5 fusion.46
  68.8 0.5 fusion.45
  69.3 14.4 %all_gather.6 = bf16[4,2,8,2048]{3,2,1,0:T(8,128)(2,1)S(1)} all-gather(bf16[1,2,8,2048]{3,2,1,0:T(8,128)(2,1)S(1)} %pad_maximum_fusion.1), channel_id=1, replica_groups=mesh['groups'=2,'freq'=4,'tile'=4] {'freq'}, dimensions={0}, use_global_device_ids=true | all-gather | bytes 327680 | tf_op jit(solution)/shard_map/all_gather | solution.py:117
  83.8 1.1 multiply_convert_fusion.1
  84.9 3.2 %fusion.8 = f32[16,8,32,8]{2,1,3,0:T(8,128)S(1)} fusion(bf16[8,16,256,1]{2,0,3,1:T(8,128)(2,1)S(1)} %bitcast.231, bf16[1,1,32,16,8,256]{5,4,3,2,1,0:T(8,128)(2,1)} %get-tuple-element.12), kind=kOutput, calls=%fused_computation.17 | convolution fusion | flops 16777216 | bytes 2293760 | tf_op jit(solution)/shard_map/ajrs,vjs->ajrv/dot_general | solution.py:63
  88.1 1.5 %fusion.9 = f32[16,8,32,8]{2,1,3,0:T(8,128)S(1)} fusion(bf16[8,16,256,1]{2,0,3,1:T(8,128)(2,1)S(1)} %bitcast.235, bf16[1,1,32,16,8,256]{5,4,3,2,1,0:T(8,128)(2,1)S(1)} %copy-done.4), kind=kOutput, calls=%fused_computation.18 | convolution fusion | flops 16777216 | bytes 2293760 | tf_op jit(solution)/shard_map/ajrs,vjs->ajrv/dot_general | solution.py:63
  89.6 1.5 %fusion.32 = bf16[1,32,16,64]{1,3,2,0:T(8,128)(2,1)S(1)} fusion(f32[16,8,32,8]{2,1,3,0:T(8,128)S(1)} %fusion.8, bf16[8,16,256,1]{2,0,3,1:T(8,128)(2,1)S(1)} %bitcast.236, bf16[1,1,32,16,8,256]{5,4,3,2,1,0:T(8,128)(2,1)S(1)} %copy-done.2), kind=kOutput, calls=%fused_computation.41 | convolution fusion | flops 16842752 | bytes 2359296 | tf_op jit(solution)/shard_map/ajrs,vjs->ajrv/dot_general | solution.py:63
  91.2 1.5 %fusion.30 = bf16[1,32,16,64]{1,3,2,0:T(8,128)(2,1)S(1)} fusion(f32[16,8,32,8]{2,1,3,0:T(8,128)S(1)} %fusion.9, bf16[8,16,256,1]{2,0,3,1:T(8,128)(2,1)S(1)} %bitcast.232, bf16[1,1,32,16,8,256]{5,4,3,2,1,0:T(8,128)(2,1)S(1)} %copy-done.2), kind=kOutput, calls=%fused_computation.39 | convolution fusion | flops 16842752 | bytes 2359296 | tf_op jit(solution)/shard_map/ajrs,vjs->ajrv/dot_general | solution.py:63
  92.7 0.2 copy.80
  93.1 0.9 reshape.622
  94.0 3.5 %all-to-all-start.1 = ((bf16[4,2,8192]{2,1,0:T(2,128)(2,1)}), bf16[4,2,8192]{2,1,0:T(2,128)(2,1)S(1)}, u32[]{:S(2)}, u32[]{:S(2)}) async-start(bf16[4,2,8192]{2,1,0:T(2,128)(2,1)} %reshape.622), calls=%async_computation.3 | async-start | bytes 262144 | tf_op jit(solution)/shard_map/all_to_all | solution.py:103
  97.6 4.4 %all-to-all-done.1 = bf16[4,2,8192]{2,1,0:T(2,128)(2,1)S(1)} async-done(((bf16[4,2,8192]{2,1,0:T(2,128)(2,1)}), bf16[4,2,8192]{2,1,0:T(2,128)(2,1)S(1)}, u32[]{:S(2)}, u32[]{:S(2)}) %all-to-all-start.1) | async-done | bytes 131104 | tf_op jit(solution)/shard_map/all_to_all | solution.py:103
  102.0 0.2 reshape.623
  102.2 0.3 copy.84
  102.6 0.3 squeeze.69
  102.8 2.1 %fusion.35 = f32[8,8,256]{2,1,0:T(8,128)S(1)} fusion(bf16[8,64,8,8]{1,3,2,0:T(8,128)(2,1)S(1)} %squeeze.69, bf16[1,1,8,64,8,256]{5,4,3,2,1,0:T(8,128)(2,1)} %get-tuple-element.10), kind=kOutput, calls=%fused_computation.44 | convolution fusion | flops 16777216 | bytes 2228224 | tf_op jit(solution)/shard_map/mdlh,mdlu->umh/dot_general | solution.py:71
  104.9 0.3 copy.83
  105.3 0.3 squeeze.68
  105.6 2.1 %fusion.36 = f32[8,8,256]{2,1,0:T(8,128)S(1)} fusion(bf16[8,64,8,8]{1,3,2,0:T(8,128)(2,1)S(1)} %squeeze.68, bf16[1,1,8,64,8,256]{5,4,3,2,1,0:T(8,128)(2,1)} %get-tuple-element.10), kind=kOutput, calls=%fused_computation.45 | convolution fusion | flops 16777216 | bytes 2228224 | tf_op jit(solution)/shard_map/mdlh,mdlu->umh/dot_general | solution.py:71
  107.7 0.5 fusion.47
  108.2 0.5 fusion.48
  108.7 14.4 %all_gather.7 = bf16[4,2,8,2048]{3,2,1,0:T(8,128)(2,1)S(1)} all-gather(bf16[1,2,8,2048]{3,2,1,0:T(8,128)(2,1)S(1)} %pad_maximum_fusion.2), channel_id=1, replica_groups=mesh['groups'=2,'freq'=4,'tile'=4] {'freq'}, dimensions={0}, use_global_device_ids=true | all-gather | bytes 327680 | tf_op jit(solution)/shard_map/all_gather | solution.py:117
  123.1 6.0 %multiply_convert_fusion = bf16[2560,2048]{1,0:T(8,128)(2,1)} fusion(bf16[128,2048]{1,0:T(8,128)(2,1)S(1)} %bitcast.224, bf16[2560,8]{0,1:T(8,128)(2,1)S(1)} %convolution_convert_fusion, s32[128]{0:T(128)S(1)} %get-tuple-element.26, s32[2560]{0:T(1024)S(1)} %add_select_fusion.1, s32[128]{0:T(128)S(1)} %get-tuple-element.25), kind=kOutput, calls=%fused_computation | convolution fusion | flops 1358889984 | bytes 11062272 | tf_op jit(solution)/shard_map/dot_general | solution.py:121
  (50 shorter events, 1.4 us)
Async XLA Ops:
  6.5 37.7 %reduce-scatter.5.cloned.1.call-start = ((), (), s32[]{:S(2)}) async-start(), calls=%async_computation.5 | async-start | bytes 1310720 | tf_op jit(solution)/shard_map/reduce_scatter | solution.py:86
  14.2 7.3 %copy-start.6 = (s32[1,32,16]{1,2,0:T(8,128)S(1)}, s32[1,32,16]{1,2,0:T(8,128)}, u32[]{:S(2)}) copy-start(s32[1,32,16]{1,2,0:T(8,128)} %param.7) | copy-start | bytes 6148
  14.2 69.5 %reduce-scatter.3.cloned.1.call-start = ((), (), s32[]{:S(2)}) async-start(), calls=%async_computation.4 | async-start | bytes 1310720 | tf_op jit(solution)/shard_map/reduce_scatter | solution.py:86
  21.9 5.1 %copy-start.5 = (bf16[1,2,8,64,8,256]{5,4,3,2,1,0:T(8,128)(2,1)S(1)}, bf16[1,2,8,64,8,256]{5,4,3,2,1,0:T(8,128)(2,1)}, u32[]{:S(2)}) copy-start(bf16[1,2,8,64,8,256]{5,4,3,2,1,0:T(8,128)(2,1)} %param.6) | copy-start | bytes 12582916
  44.2 4.4 %copy-start.3 = (bf16[1,1,32,16,8,256]{5,4,3,2,1,0:T(8,128)(2,1)S(1)}, bf16[1,1,32,16,8,256]{5,4,3,2,1,0:T(8,128)(2,1)}, u32[]{:S(2)}) copy-start(bf16[1,1,32,16,8,256]{5,4,3,2,1,0:T(8,128)(2,1)} %get-tuple-element.12) | copy-start | bytes 6291460
  45.3 4.7 %copy-start.1 = (bf16[1,1,32,16,8,256]{5,4,3,2,1,0:T(8,128)(2,1)S(1)}, bf16[1,1,32,16,8,256]{5,4,3,2,1,0:T(8,128)(2,1)}, u32[]{:S(2)}) copy-start(bf16[1,1,32,16,8,256]{5,4,3,2,1,0:T(8,128)(2,1)} %get-tuple-element.11) | copy-start | bytes 6291460
  56.1 7.9 %all-to-all-start = ((bf16[4,2,8192]{2,1,0:T(2,128)(2,1)}), bf16[4,2,8192]{2,1,0:T(2,128)(2,1)S(1)}, u32[]{:S(2)}, u32[]{:S(2)}) async-start(bf16[4,2,8192]{2,1,0:T(2,128)(2,1)} %reshape.620), calls=%async_computation.2 | async-start | bytes 262144 | tf_op jit(solution)/shard_map/all_to_all | solution.py:103
  65.5 2.3 %copy-start = (bf16[1,1,8,64,8,256]{5,4,3,2,1,0:T(8,128)(2,1)S(1)}, bf16[1,1,8,64,8,256]{5,4,3,2,1,0:T(8,128)(2,1)}, u32[]{:S(2)}) copy-start(bf16[1,1,8,64,8,256]{5,4,3,2,1,0:T(8,128)(2,1)} %get-tuple-element.10) | copy-start | bytes 6291460
  83.8 4.4 %copy-start.4 = (bf16[1,1,32,16,8,256]{5,4,3,2,1,0:T(8,128)(2,1)S(1)}, bf16[1,1,32,16,8,256]{5,4,3,2,1,0:T(8,128)(2,1)}, u32[]{:S(2)}) copy-start(bf16[1,1,32,16,8,256]{5,4,3,2,1,0:T(8,128)(2,1)} %get-tuple-element.12) | copy-start | bytes 6291460
  84.9 4.7 %copy-start.2 = (bf16[1,1,32,16,8,256]{5,4,3,2,1,0:T(8,128)(2,1)S(1)}, bf16[1,1,32,16,8,256]{5,4,3,2,1,0:T(8,128)(2,1)}, u32[]{:S(2)}) copy-start(bf16[1,1,32,16,8,256]{5,4,3,2,1,0:T(8,128)(2,1)} %get-tuple-element.11) | copy-start | bytes 6291460
  94.0 7.9 %all-to-all-start.1 = ((bf16[4,2,8192]{2,1,0:T(2,128)(2,1)}), bf16[4,2,8192]{2,1,0:T(2,128)(2,1)S(1)}, u32[]{:S(2)}, u32[]{:S(2)}) async-start(bf16[4,2,8192]{2,1,0:T(2,128)(2,1)} %reshape.622), calls=%async_computation.3 | async-start | bytes 262144 | tf_op jit(solution)/shard_map/all_to_all | solution.py:103
Sparse Core Ops, SparseCore 0:
  14.3 29.8 reduce-scatter.4
  46.6 25.7 reduce-scatter.2
where the time goes:
time: 137 us; the launch traced here: 136 us
  matrix products  47.6 us (35%)
  blocking collectives  28.8 us (21%)
  waiting for transfers between devices  23 us (17%)
  between operations  13.8 us (10%)
  local copies, waits for them, and re-layouts  12.6 us (9%)
  starting transfers between devices  7.09 us (5%)
  other arithmetic  3.11 us (2%)
    all_gather x2, blocking collectives, per_device(): pieces.append(lax.all_gather(received, 'freq', axis=0, tiled=True))  28.8 us
    dot_general x8, matrix products, source_product(): jnp.einsum('ajrs,vjs->ajrv', left_operand_factors, right_operand_factors,...  17.1 us
    reduce_scatter x2, waiting for transfers between devices, per_device(): lax.psum_scatter(partial, 'freq', scatter_dimension=0, tiled=True)  14.2 us
    dot_general x2, matrix products, per_device(): jnp.dot(forward, flat_traces, preferred_element_type=jnp.float32)  13.8 us
    dot_general x8, matrix products, receiver_product(): jnp.einsum('mdlh,mdlu->umh', left_operand_factors, right_operand_factors,...  8.98 us
    all_to_all x2, waiting for transfers between devices, per_device(): lax.all_to_all(coefficients, 'tile', split_axis=1, concat_axis=2, tiled=T...  8.77 us
    all_to_all x2, starting transfers between devices, per_device(): lax.all_to_all(coefficients, 'tile', split_axis=1, concat_axis=2, tiled=T...  7.05 us
    dot_general x1, matrix products, per_device(): jnp.dot(spread_over(backward, virtual_sources), piece.reshape(count * 2 *...  6.02 us
  transfers between devices with their start and end apart: 4, of which 3 were waited for; matrix products, arithmetic and copies ran while one was open for 24% of the time, Pallas kernels for 0%

commit v1 on v0

--- a/solution.py
+++ b/solution.py
@@ -100,7 +100,15 @@
         stacked = jnp.stack([real_coeff, imag_coeff])
         coefficients = jnp.where(rank_mask[None], stacked, jnp.float32(0.0)).astype(jnp.bfloat16)
         coefficients = coefficients.reshape(2, rows_all, columns, rank_positions * width)
-        arrived = lax.all_to_all(coefficients, "tile", split_axis=1, concat_axis=2, tiled=True)
+        arrived = jnp.concatenate(
+            lax.all_to_all(
+                jnp.stack(jnp.split(coefficients, lax.psum(1, axis_name="tile"), axis=1), axis=0),
+                axis_name="tile",
+                split_axis=0,
+                concat_axis=0,
+            ),
+            axis=2,
+        )
         rows_local = arrived.shape[1]
         columns_all = arrived.shape[2]
         arrived = arrived.reshape(2, rows_local, columns_all, rank_positions, width)

time: 137 us -> 137 us (level)
  no operation moved by 1% of the time
where the time goes in v1:
time: 137 us; the launch traced here: 136 us
  matrix products  47.6 us (35%)
  blocking collectives  28.8 us (21%)
  waiting for transfers between devices  23 us (17%)
  between operations  13.8 us (10%)
  local copies, waits for them, and re-layouts  12.5 us (9%)
  starting transfers between devices  7.09 us (5%)
  other arithmetic  3.22 us (2%)
    all_gather x2, blocking collectives, per_device(): pieces.append(lax.all_gather(received, 'freq', axis=0, tiled=True))  28.8 us
    dot_general x8, matrix products, source_product(): jnp.einsum('ajrs,vjs->ajrv', left_operand_factors, right_operand_factors,...  17.1 us
    reduce_scatter x2, waiting for transfers between devices, per_device(): lax.psum_scatter(partial, 'freq', scatter_dimension=0, tiled=True)  14.2 us
    dot_general x2, matrix products, per_device(): jnp.dot(forward, flat_traces, preferred_element_type=jnp.float32)  13.8 us
    dot_general x8, matrix products, receiver_product(): jnp.einsum('mdlh,mdlu->umh', left_operand_factors, right_operand_factors,...  8.98 us
    all_to_all x2, waiting for transfers between devices, per_device(): lax.all_to_all(jnp.stack(jnp.split(coefficients, lax.psum(1, axis_name='t...  8.77 us
    all_to_all x2, starting transfers between devices, per_device(): lax.all_to_all(jnp.stack(jnp.split(coefficients, lax.psum(1, axis_name='t...  7.05 us
    dot_general x1, matrix products, per_device(): jnp.dot(spread_over(backward, virtual_sources), piece.reshape(count * 2 *...  6.02 us
  transfers between devices with their start and end apart: 4, of which 3 were waited for; matrix products, arithmetic and copies ran while one was open for 24% of the time, Pallas kernels for 0%

profile of v1, /device:TPU:0, one launch (start us, length us, event | category | flops | bytes accessed | tf_op | source)
XLA Modules:
  0.0 136.1 jit_solution(8615095730629220018)
XLA Ops:
  6.9 0.4 fusion.7
  7.3 6.9 %fusion = f32[4,2,8,4096]{3,2,1,0:T(8,128)} fusion(bf16[4,2,8,1280]{3,2,1,0:T(8,128)(2,1)S(1)} %bitcast.246, bf16[160,16,4096]{2,1,0:T(8,128)(2,1)} %param.4), kind=kOutput, calls=%fused_computation.1 | convolution fusion | flops 671088640 | bytes 11698176 | tf_op jit(solution)/shard_map/dot_general | solution.py:83
  14.3 6.9 %fusion.2 = f32[4,2,8,4096]{3,2,1,0:T(8,128)} fusion(bf16[4,2,8,1280]{3,2,1,0:T(8,128)(2,1)S(1)} %bitcast.247, bf16[160,16,4096]{2,1,0:T(8,128)(2,1)} %param.4), kind=kOutput, calls=%fused_computation.3 | convolution fusion | flops 671088640 | bytes 11698176 | tf_op jit(solution)/shard_map/dot_general | solution.py:83
  21.6 0.2 copy.82
  21.9 5.1 %fusion.83 = (bf16[1,1,32,16,8,256]{5,4,3,2,1,0:T(8,128)(2,1)}, bf16[1,1,32,16,8,256]{5,4,3,2,1,0:T(8,128)(2,1)}) fusion(bf16[1,2,32,16,8,256]{5,4,3,2,1,0:T(8,128)(2,1)} %param.5), kind=kLoop, calls=%fused_computation.145 | loop fusion | bytes 8388608 | tf_op jit(solution)/shard_map/slice | solution.py:95
  27.0 1.6 %fusion.82 = (bf16[1,1,8,64,8,256]{5,4,3,2,1,0:T(8,128)(2,1)S(1)}, bf16[1,1,8,64,8,256]{5,4,3,2,1,0:T(8,128)(2,1)}) fusion(bf16[1,2,8,64,8,256]{5,4,3,2,1,0:T(8,128)(2,1)S(1)} %copy-done.5), kind=kLoop, calls=%fused_computation.144 | loop fusion | bytes 8388608 | tf_op jit(solution)/shard_map/slice | solution.py:115
  28.6 1.4 %convolution_convert_fusion = bf16[2560,8]{0,1:T(8,128)(2,1)S(1)} fusion(bf16[160,8]{0,1:T(8,128)(2,1)S(1)} %reshape.602, s32[2560]{0:T(1024)S(1)} %add_select_fusion), kind=kOutput, calls=%fused_computation.9 | convolution fusion | flops 6983680 | bytes 53760 | tf_op jit(solution)/shard_map/dot_general | solution.py:29
  30.0 14.2 %reduce-scatter.5.cloned.1.call-done = f32[1,2,8,4096]{3,2,1,0:T(8,128)} async-done(((f32[4,2,8,4096]{3,2,1,0:T(8,128)}), f32[1,2,8,4096]{3,2,1,0:T(8,128)}) %reduce-scatter.5.cloned.1.call-update) | async-done | bytes 262160 | tf_op jit(solution)/shard_map/reduce_scatter | solution.py:86
  44.2 1.1 multiply_convert_fusion.2
  45.3 3.2 %fusion.10 = f32[16,8,32,8]{2,1,3,0:T(8,128)S(1)} fusion(bf16[8,16,256,1]{2,0,3,1:T(8,128)(2,1)S(1)} %bitcast.233, bf16[1,1,32,16,8,256]{5,4,3,2,1,0:T(8,128)(2,1)} %get-tuple-element.12), kind=kOutput, calls=%fused_computation.19 | convolution fusion | flops 16777216 | bytes 2293760 | tf_op jit(solution)/shard_map/ajrs,vjs->ajrv/dot_general | solution.py:63
  48.6 1.5 %fusion.11 = f32[16,8,32,8]{2,1,3,0:T(8,128)S(1)} fusion(bf16[8,16,256,1]{2,0,3,1:T(8,128)(2,1)S(1)} %bitcast.237, bf16[1,1,32,16,8,256]{5,4,3,2,1,0:T(8,128)(2,1)S(1)} %copy-done.3), kind=kOutput, calls=%fused_computation.20 | convolution fusion | flops 16777216 | bytes 2293760 | tf_op jit(solution)/shard_map/ajrs,vjs->ajrv/dot_general | solution.py:63
  50.1 1.5 %fusion.28 = bf16[1,32,16,64]{1,3,2,0:T(8,128)(2,1)S(1)} fusion(f32[16,8,32,8]{2,1,3,0:T(8,128)S(1)} %fusion.10, bf16[8,16,256,1]{2,0,3,1:T(8,128)(2,1)S(1)} %bitcast.238, bf16[1,1,32,16,8,256]{5,4,3,2,1,0:T(8,128)(2,1)S(1)} %copy-done.1), kind=kOutput, calls=%fused_computation.37 | convolution fusion | flops 16842752 | bytes 2359296 | tf_op jit(solution)/shard_map/ajrs,vjs->ajrv/dot_general | solution.py:63
  51.6 0.2 copy.86
  51.8 3.1 %fusion.26 = bf16[1,32,16,64]{1,3,2,0:T(8,128)(2,1)S(1)} fusion(f32[16,8,32,8]{2,1,3,0:T(8,128)S(1)} %fusion.11, bf16[8,16,256,1]{2,0,3,1:T(8,128)(2,1)S(1)} %bitcast.234, bf16[1,1,32,16,8,256]{5,4,3,2,1,0:T(8,128)(2,1)} %get-tuple-element.11), kind=kOutput, calls=%fused_computation.35 | convolution fusion | flops 16842752 | bytes 2359296 | tf_op jit(solution)/shard_map/ajrs,vjs->ajrv/dot_general | solution.py:63
  54.9 0.2 copy.85
  55.3 0.9 reshape.624
  56.2 3.5 %all-to-all-start = ((bf16[4,2,8192]{2,1,0:T(2,128)(2,1)}), bf16[4,2,8192]{2,1,0:T(2,128)(2,1)S(1)}, u32[]{:S(2)}, u32[]{:S(2)}) async-start(bf16[4,2,8192]{2,1,0:T(2,128)(2,1)} %reshape.624), calls=%async_computation.2 | async-start | bytes 262144 | tf_op jit(solution)/shard_map/all_to_all | solution.py:104
  59.7 4.4 %all-to-all-done = bf16[4,2,8192]{2,1,0:T(2,128)(2,1)S(1)} async-done(((bf16[4,2,8192]{2,1,0:T(2,128)(2,1)}), bf16[4,2,8192]{2,1,0:T(2,128)(2,1)S(1)}, u32[]{:S(2)}, u32[]{:S(2)}) %all-to-all-start) | async-done | bytes 131104 | tf_op jit(solution)/shard_map/all_to_all | solution.py:104
  64.1 0.2 reshape.625
  64.4 0.3 copy.89
  64.7 0.3 squeeze.30
  65.0 0.3 copy.87
  65.3 0.3 squeeze.28
  65.6 2.2 %fusion.34 = f32[8,8,256]{2,1,0:T(8,128)S(1)} fusion(bf16[8,64,8,8]{1,3,2,0:T(8,128)(2,1)S(1)} %squeeze.28, bf16[1,1,8,64,8,256]{5,4,3,2,1,0:T(8,128)(2,1)} %get-tuple-element.10), kind=kOutput, calls=%fused_computation.43 | convolution fusion | flops 16777216 | bytes 2228224 | tf_op jit(solution)/shard_map/mdlh,mdlu->umh/dot_general | solution.py:71
  67.8 0.5 fusion.33
  68.3 0.5 fusion.46
  68.8 0.5 fusion.45
  69.4 14.4 %all_gather.6 = bf16[4,2,8,2048]{3,2,1,0:T(8,128)(2,1)S(1)} all-gather(bf16[1,2,8,2048]{3,2,1,0:T(8,128)(2,1)S(1)} %pad_maximum_fusion.3), channel_id=1, replica_groups=mesh['groups'=2,'freq'=4,'tile'=4] {'freq'}, dimensions={0}, use_global_device_ids=true | all-gather | bytes 327680 | tf_op jit(solution)/shard_map/all_gather | solution.py:125
  83.8 1.1 multiply_convert_fusion.1
  85.0 3.2 %fusion.8 = f32[16,8,32,8]{2,1,3,0:T(8,128)S(1)} fusion(bf16[8,16,256,1]{2,0,3,1:T(8,128)(2,1)S(1)} %bitcast.235, bf16[1,1,32,16,8,256]{5,4,3,2,1,0:T(8,128)(2,1)} %get-tuple-element.12), kind=kOutput, calls=%fused_computation.17 | convolution fusion | flops 16777216 | bytes 2293760 | tf_op jit(solution)/shard_map/ajrs,vjs->ajrv/dot_general | solution.py:63
  88.2 1.5 %fusion.9 = f32[16,8,32,8]{2,1,3,0:T(8,128)S(1)} fusion(bf16[8,16,256,1]{2,0,3,1:T(8,128)(2,1)S(1)} %bitcast.239, bf16[1,1,32,16,8,256]{5,4,3,2,1,0:T(8,128)(2,1)S(1)} %copy-done.4), kind=kOutput, calls=%fused_computation.18 | convolution fusion | flops 16777216 | bytes 2293760 | tf_op jit(solution)/shard_map/ajrs,vjs->ajrv/dot_general | solution.py:63
  89.7 1.5 %fusion.32 = bf16[1,32,16,64]{1,3,2,0:T(8,128)(2,1)S(1)} fusion(f32[16,8,32,8]{2,1,3,0:T(8,128)S(1)} %fusion.8, bf16[8,16,256,1]{2,0,3,1:T(8,128)(2,1)S(1)} %bitcast.240, bf16[1,1,32,16,8,256]{5,4,3,2,1,0:T(8,128)(2,1)S(1)} %copy-done.2), kind=kOutput, calls=%fused_computation.41 | convolution fusion | flops 16842752 | bytes 2359296 | tf_op jit(solution)/shard_map/ajrs,vjs->ajrv/dot_general | solution.py:63
  91.2 1.5 %fusion.30 = bf16[1,32,16,64]{1,3,2,0:T(8,128)(2,1)S(1)} fusion(f32[16,8,32,8]{2,1,3,0:T(8,128)S(1)} %fusion.9, bf16[8,16,256,1]{2,0,3,1:T(8,128)(2,1)S(1)} %bitcast.236, bf16[1,1,32,16,8,256]{5,4,3,2,1,0:T(8,128)(2,1)S(1)} %copy-done.2), kind=kOutput, calls=%fused_computation.39 | convolution fusion | flops 16842752 | bytes 2359296 | tf_op jit(solution)/shard_map/ajrs,vjs->ajrv/dot_general | solution.py:63
  92.7 0.2 copy.91
  93.3 0.9 reshape.626
  94.2 3.5 %all-to-all-start.1 = ((bf16[4,2,8192]{2,1,0:T(2,128)(2,1)}), bf16[4,2,8192]{2,1,0:T(2,128)(2,1)S(1)}, u32[]{:S(2)}, u32[]{:S(2)}) async-start(bf16[4,2,8192]{2,1,0:T(2,128)(2,1)} %reshape.626), calls=%async_computation.3 | async-start | bytes 262144 | tf_op jit(solution)/shard_map/all_to_all | solution.py:104
  97.8 4.4 %all-to-all-done.1 = bf16[4,2,8192]{2,1,0:T(2,128)(2,1)S(1)} async-done(((bf16[4,2,8192]{2,1,0:T(2,128)(2,1)}), bf16[4,2,8192]{2,1,0:T(2,128)(2,1)S(1)}, u32[]{:S(2)}, u32[]{:S(2)}) %all-to-all-start.1) | async-done | bytes 131104 | tf_op jit(solution)/shard_map/all_to_all | solution.py:104
  102.1 0.2 reshape.627
  102.4 0.3 copy.94
  102.7 0.3 squeeze.69
  103.0 2.1 %fusion.35 = f32[8,8,256]{2,1,0:T(8,128)S(1)} fusion(bf16[8,64,8,8]{1,3,2,0:T(8,128)(2,1)S(1)} %squeeze.69, bf16[1,1,8,64,8,256]{5,4,3,2,1,0:T(8,128)(2,1)} %get-tuple-element.10), kind=kOutput, calls=%fused_computation.44 | convolution fusion | flops 16777216 | bytes 2228224 | tf_op jit(solution)/shard_map/mdlh,mdlu->umh/dot_general | solution.py:71
  105.1 0.3 copy.93
  105.4 0.3 squeeze.68
  105.7 2.1 %fusion.36 = f32[8,8,256]{2,1,0:T(8,128)S(1)} fusion(bf16[8,64,8,8]{1,3,2,0:T(8,128)(2,1)S(1)} %squeeze.68, bf16[1,1,8,64,8,256]{5,4,3,2,1,0:T(8,128)(2,1)} %get-tuple-element.10), kind=kOutput, calls=%fused_computation.45 | convolution fusion | flops 16777216 | bytes 2228224 | tf_op jit(solution)/shard_map/mdlh,mdlu->umh/dot_general | solution.py:71
  107.8 0.5 fusion.47
  108.3 0.5 fusion.48
  108.8 14.4 %all_gather.7 = bf16[4,2,8,2048]{3,2,1,0:T(8,128)(2,1)S(1)} all-gather(bf16[1,2,8,2048]{3,2,1,0:T(8,128)(2,1)S(1)} %pad_maximum_fusion.4), channel_id=1, replica_groups=mesh['groups'=2,'freq'=4,'tile'=4] {'freq'}, dimensions={0}, use_global_device_ids=true | all-gather | bytes 327680 | tf_op jit(solution)/shard_map/all_gather | solution.py:125
  123.3 6.0 %multiply_convert_fusion = bf16[2560,2048]{1,0:T(8,128)(2,1)} fusion(bf16[128,2048]{1,0:T(8,128)(2,1)S(1)} %bitcast.230, bf16[2560,8]{0,1:T(8,128)(2,1)S(1)} %convolution_convert_fusion, s32[128]{0:T(128)S(1)} %get-tuple-element.34, s32[2560]{0:T(1024)S(1)} %add_select_fusion.1, s32[128]{0:T(128)S(1)} %get-tuple-element.33), kind=kOutput, calls=%fused_computation | convolution fusion | flops 1358889984 | bytes 11062272 | tf_op jit(solution)/shard_map/dot_general | solution.py:129
  (52 shorter events, 1.5 us)
Async XLA Ops:
  6.5 37.7 %reduce-scatter.5.cloned.1.call-start = ((), (), s32[]{:S(2)}) async-start(), calls=%async_computation.5 | async-start | bytes 1310720 | tf_op jit(solution)/shard_map/reduce_scatter | solution.py:86
  14.2 7.3 %copy-start.6 = (s32[1,32,16]{1,2,0:T(8,128)S(1)}, s32[1,32,16]{1,2,0:T(8,128)}, u32[]{:S(2)}) copy-start(s32[1,32,16]{1,2,0:T(8,128)} %param.7) | copy-start | bytes 6148
  14.2 69.6 %reduce-scatter.3.cloned.1.call-start = ((), (), s32[]{:S(2)}) async-start(), calls=%async_computation.4 | async-start | bytes 1310720 | tf_op jit(solution)/shard_map/reduce_scatter | solution.py:86
  21.9 5.1 %copy-start.5 = (bf16[1,2,8,64,8,256]{5,4,3,2,1,0:T(8,128)(2,1)S(1)}, bf16[1,2,8,64,8,256]{5,4,3,2,1,0:T(8,128)(2,1)}, u32[]{:S(2)}) copy-start(bf16[1,2,8,64,8,256]{5,4,3,2,1,0:T(8,128)(2,1)} %param.6) | copy-start | bytes 12582916
  44.2 4.4 %copy-start.3 = (bf16[1,1,32,16,8,256]{5,4,3,2,1,0:T(8,128)(2,1)S(1)}, bf16[1,1,32,16,8,256]{5,4,3,2,1,0:T(8,128)(2,1)}, u32[]{:S(2)}) copy-start(bf16[1,1,32,16,8,256]{5,4,3,2,1,0:T(8,128)(2,1)} %get-tuple-element.12) | copy-start | bytes 6291460
  45.3 4.7 %copy-start.1 = (bf16[1,1,32,16,8,256]{5,4,3,2,1,0:T(8,128)(2,1)S(1)}, bf16[1,1,32,16,8,256]{5,4,3,2,1,0:T(8,128)(2,1)}, u32[]{:S(2)}) copy-start(bf16[1,1,32,16,8,256]{5,4,3,2,1,0:T(8,128)(2,1)} %get-tuple-element.11) | copy-start | bytes 6291460
  56.2 7.9 %all-to-all-start = ((bf16[4,2,8192]{2,1,0:T(2,128)(2,1)}), bf16[4,2,8192]{2,1,0:T(2,128)(2,1)S(1)}, u32[]{:S(2)}, u32[]{:S(2)}) async-start(bf16[4,2,8192]{2,1,0:T(2,128)(2,1)} %reshape.624), calls=%async_computation.2 | async-start | bytes 262144 | tf_op jit(solution)/shard_map/all_to_all | solution.py:104
  65.6 2.3 %copy-start = (bf16[1,1,8,64,8,256]{5,4,3,2,1,0:T(8,128)(2,1)S(1)}, bf16[1,1,8,64,8,256]{5,4,3,2,1,0:T(8,128)(2,1)}, u32[]{:S(2)}) copy-start(bf16[1,1,8,64,8,256]{5,4,3,2,1,0:T(8,128)(2,1)} %get-tuple-element.10) | copy-start | bytes 6291460
  83.8 4.4 %copy-start.4 = (bf16[1,1,32,16,8,256]{5,4,3,2,1,0:T(8,128)(2,1)S(1)}, bf16[1,1,32,16,8,256]{5,4,3,2,1,0:T(8,128)(2,1)}, u32[]{:S(2)}) copy-start(bf16[1,1,32,16,8,256]{5,4,3,2,1,0:T(8,128)(2,1)} %get-tuple-element.12) | copy-start | bytes 6291460
  85.0 4.7 %copy-start.2 = (bf16[1,1,32,16,8,256]{5,4,3,2,1,0:T(8,128)(2,1)S(1)}, bf16[1,1,32,16,8,256]{5,4,3,2,1,0:T(8,128)(2,1)}, u32[]{:S(2)}) copy-start(bf16[1,1,32,16,8,256]{5,4,3,2,1,0:T(8,128)(2,1)} %get-tuple-element.11) | copy-start | bytes 6291460
  94.2 7.9 %all-to-all-start.1 = ((bf16[4,2,8192]{2,1,0:T(2,128)(2,1)}), bf16[4,2,8192]{2,1,0:T(2,128)(2,1)S(1)}, u32[]{:S(2)}, u32[]{:S(2)}) async-start(bf16[4,2,8192]{2,1,0:T(2,128)(2,1)} %reshape.626), calls=%async_computation.3 | async-start | bytes 262144 | tf_op jit(solution)/shard_map/all_to_all | solution.py:104
Sparse Core Ops, SparseCore 0:
  14.3 29.8 reduce-scatter.4
  46.6 25.7 reduce-scatter.2
